TPU v7x, 256 devices: a whole 4x4x8 slice. The times are simulated.
256 devices in a mesh: layer: 2 (over core), feat: 4 (over x), tok: 32 (over z, y).
Axes of the slice: x: 4, y: 4, z: 8, core: 2. Of those that a mesh axis runs over, the one named last changes fastest.
Arguments:
- resid_in: bfloat16 [8192, 2304], P('tok', 'feat'), may hold values from -6 to 6
- attn_out: bfloat16 [2, 8192, 2304], P('layer', 'tok', 'feat'), may hold values from -4 to 4
- carry_in: bfloat16 [8192, 2304], P('tok', 'feat'), may hold values from -4 to 4
- enc_weight: bfloat16 [2, 2304, 8192], P('layer', None, 'feat'), may hold values from -0.125 to 0.125
- enc_bias: float32 [2, 8192], P('layer', 'feat'), may hold values from -3 to 3
- dec_own: bfloat16 [2, 8192, 2304], P('layer', 'feat', 'tok'), may hold values from -0.125 to 0.125
- dec_next: bfloat16 [2, 8192, 2304], P('layer', 'feat', 'tok'), may hold values from -0.125 to 0.125
- block_list: int32 [2, 64, 32], P('layer', 'tok'), may hold values from 0 to 63, all different within a row
- block_count: int32 [2, 64], P('layer', 'tok'), may hold values from 8 to 32, as said below
Outputs:
- reconstruction: bfloat16 [2, 8192, 2304], P('layer', 'tok', 'feat')
- outgoing: bfloat16 [2, 8192, 2304], P('layer', 'tok', 'feat')
Inputs may be any that keep to these rules, and one draw needn't show every extreme that they name: Each row of block_list names 32 different blocks; only its first block_count entries are in use. `block_count`: some entry equals 32.
All inputs are finite; a program needn't handle non-finite values.
Results may differ from a plain program's by a relative error of at most 0.015.
Values may be sent and summed in bfloat16 or wider, within the bound.
No kernel may reach another device: no remote copies, remote signals or barrier semaphores. Data moves between devices by JAX's collectives and lax.ppermute only.
A program may use at most 128 MiB of HBM per device.

v0:
```python
import jax
import jax.numpy as jnp
from jax import lax
from jax.sharding import PartitionSpec as P

BLOCK = 128
TILE = 128
GROUP = ("layer", "feat")


def within_layer(shard, section, shift, n_feat):
    if section is None:
        return lax.ppermute(shard, "feat", [(i, (i + shift) % n_feat) for i in range(n_feat)])
    pairs = [(section * n_feat + i, section * n_feat + (i + shift) % n_feat) for i in range(n_feat)]
    return lax.ppermute(shard, GROUP, pairs)


def feat_gather(part, section, feat_index, n_feat):
    received = [part] + [within_layer(part, section, k, n_feat) for k in range(1, n_feat)]
    blocks = []
    for j in range(n_feat):
        block = jnp.zeros_like(part)
        for k in range(n_feat):
            block = jnp.where((feat_index - k) % n_feat == j, received[k], block)
        blocks.append(block)
    return jnp.concatenate(blocks, axis=-1)


def feat_reduce_scatter(terms, section, feat_index, n_feat):
    cols = terms.shape[-1] // n_feat
    total = lax.dynamic_slice_in_dim(terms, feat_index * cols, cols, terms.ndim - 1).astype(
        jnp.float32
    )
    for k in range(1, n_feat):
        target = (feat_index + k) % n_feat
        piece = lax.dynamic_slice_in_dim(terms, target * cols, cols, terms.ndim - 1)
        total = total + within_layer(piece, section, k, n_feat).astype(jnp.float32)
    return total


def decode_scatter(features, decoder, feat_index, n_feat):
    cols = decoder.shape[1] // n_feat
    total = None
    for k in sorted(range(n_feat), key=lambda shift: (-min(shift, n_feat - shift), shift)):
        target = (feat_index + k) % n_feat
        chunk = lax.dynamic_slice_in_dim(decoder, target * cols, cols, 1)
        piece = jnp.dot(features, chunk, preferred_element_type=jnp.float32).astype(jnp.bfloat16)
        if k:
            piece = within_layer(piece, None, k, n_feat)
        else:
            piece = lax.optimization_barrier(piece)
        piece = piece.astype(jnp.float32)
        total = piece if total is None else total + piece
    return total


def feature_mask(block_list, block_count, feat_index, blocks_dev):
    listed = block_list[0]
    in_use = jnp.arange(listed.shape[1], dtype=jnp.int32)[None, :] < block_count[0][:, None]
    own_blocks = feat_index * blocks_dev + jnp.arange(blocks_dev, dtype=jnp.int32)
    matches = (listed[:, None, :] == own_blocks[None, :, None]) & in_use[:, None, :]
    active = jnp.any(matches, axis=2).astype(jnp.float32)
    return jnp.repeat(jnp.repeat(active, TILE, axis=0), BLOCK, axis=1)


def encode(gathered, enc_weight, enc_bias, mask):
    preact = (
        jnp.dot(gathered, enc_weight[0], preferred_element_type=jnp.float32) + enc_bias[0][None, :]
    )
    return (jax.nn.relu(preact) * mask).astype(jnp.bfloat16)


def shards(
    resid_in, attn_out, carry_in, enc_weight, enc_bias, dec_own, dec_next, block_list, block_count
):
    n_feat = lax.axis_size("feat")
    section_index = lax.axis_index("layer")
    feat_index = lax.axis_index("feat")
    blocks_dev = enc_weight.shape[2] // BLOCK
    first_core = section_index == 0
    swapped_next = lax.ppermute(dec_next[0], "layer", [(0, 1), (1, 0)])
    first_dec = jnp.where(first_core, dec_own[0], swapped_next)
    second_dec = jnp.where(first_core, swapped_next, dec_own[0])
    first_full = lax.all_gather(first_dec, "tok", axis=1, tiled=True)
    second_full = lax.all_gather(second_dec, "tok", axis=1, tiled=True)
    mask = feature_mask(block_list, block_count, feat_index, blocks_dev)
    attention = attn_out[0].astype(jnp.float32)
    gathered = feat_gather(resid_in, 0, feat_index, n_feat)
    features = lax.cond(
        first_core,
        lambda source: encode(source, enc_weight, enc_bias, mask),
        lambda source: jnp.zeros((source.shape[0], enc_weight.shape[2]), jnp.bfloat16),
        gathered,
    )
    features = jnp.where(first_core, features, lax.ppermute(features, "layer", [(0, 1)]))
    summed = decode_scatter(features, first_full, feat_index, n_feat)
    recon_first = summed + carry_in.astype(jnp.float32)
    residual_next = (resid_in.astype(jnp.float32) + attention + recon_first).astype(jnp.bfloat16)
    outgoing_first = summed.astype(jnp.bfloat16)
    swapped = lax.ppermute(
        jnp.where(first_core, residual_next, outgoing_first), "layer", [(0, 1), (1, 0)]
    )
    gathered = feat_gather(swapped, 1, feat_index, n_feat)
    features = lax.cond(
        first_core,
        lambda source: jnp.zeros((source.shape[0], enc_weight.shape[2]), jnp.bfloat16),
        lambda source: encode(source, enc_weight, enc_bias, mask),
        gathered,
    )
    features = jnp.where(first_core, lax.ppermute(features, "layer", [(1, 0)]), features)
    summed = decode_scatter(features, second_full, feat_index, n_feat)
    recon_second = summed + outgoing_first.astype(jnp.float32)
    outgoing_second = lax.ppermute(summed.astype(jnp.bfloat16), "layer", [(0, 1)])
    recon_out = jnp.where(first_core, recon_first, recon_second).astype(jnp.bfloat16)
    outgoing_out = jnp.where(first_core, swapped, outgoing_second)
    return (recon_out[None], outgoing_out[None])


def solution(mesh):
    return jax.shard_map(
        shards,
        mesh=mesh,
        in_specs=(
            P("tok", "feat"),
            P("layer", "tok", "feat"),
            P("tok", "feat"),
            P("layer", None, "feat"),
            P("layer", "feat"),
            P("layer", "feat", "tok"),
            P("layer", "feat", "tok"),
            P("layer", "tok", None),
            P("layer", "tok"),
        ),
        out_specs=(P("layer", "tok", "feat"), P("layer", "tok", "feat")),
        check_vma=False,
    )
```

profile of v0, /device:TPU:7, one launch (start us, length us, event | category | flops | bytes accessed | tf_op | source)
XLA Modules:
  0.0 253.3 jit_solution(8539006567864455377)
XLA Ops:
  19.6 19.7 %collective-permute-done.3 = bf16[256,2048]{1,0:T(8,128)(2,1)} collective-permute-done((bf16[256,2048]{1,0:T(8,128)(2,1)S(1)}, bf16[256,2048]{1,0:T(8,128)(2,1)}, u32[]{:S(2)}, u32[]{:S(2)}) %collective-permute-start.3) | collective-permute-done | bytes 1048608 | tf_op jit(solution)/shard_map/ppermute | solution.py:95
  39.3 2.3 broadcast_select_fusion.1
  41.6 74.9 %all-gather.3.cloned.1.call-done = bf16[2048,2304]{0,1:T(8,128)(2,1)} async-done(((bf16[2048,72]{0,1:T(8,128)(2,1)}), bf16[2048,2304]{0,1:T(8,128)(2,1)}) %all-gather.3.cloned.1.call-update) | async-done | bytes 9437200 | tf_op jit(solution)/shard_map/all_gather | solution.py:84
  116.5 3.6 %fusion.44 = bf16[256,576]{0,1:T(8,128)(2,1)} fusion(bf16[256,2048]{1,0:T(8,128)(2,1)} %broadcast_select_fusion.1, bf16[2048,2304]{0,1:T(8,128)(2,1)} %all-gather.3.cloned.1.call-done, s32[]{:T(128)S(6)} %select_n.357), kind=kOutput, calls=%fused_computation.29 | convolution fusion | flops 604127232 | bytes 3702788 | tf_op jit(solution)/shard_map/dot_general | solution.py:47
  121.3 3.3 %fusion.47 = bf16[256,576]{0,1:T(8,128)(2,1)} fusion(bf16[256,2048]{1,0:T(8,128)(2,1)S(1)} %copy-done.9, bf16[2048,2304]{0,1:T(8,128)(2,1)} %all-gather.3.cloned.1.call-done, s32[]{:T(128)S(6)} %select_n.359), kind=kOutput, calls=%fused_computation.30 | convolution fusion | flops 604127232 | bytes 3702788 | tf_op jit(solution)/shard_map/dot_general | solution.py:47
  126.4 3.3 %fusion.50 = bf16[256,576]{0,1:T(8,128)(2,1)} fusion(bf16[256,2048]{1,0:T(8,128)(2,1)S(1)} %copy-done.9, bf16[2048,2304]{0,1:T(8,128)(2,1)} %all-gather.3.cloned.1.call-done, s32[]{:T(128)S(6)} %select_n.361), kind=kOutput, calls=%fused_computation.31 | convolution fusion | flops 604127232 | bytes 3702788 | tf_op jit(solution)/shard_map/dot_general | solution.py:47
  129.6 3.0 %fusion.53 = bf16[256,576]{0,1:T(8,128)(2,1)S(1)} fusion(bf16[256,2048]{1,0:T(8,128)(2,1)} %broadcast_select_fusion.1, bf16[2048,2304]{0,1:T(8,128)(2,1)} %all-gather.3.cloned.1.call-done, s32[]{:T(128)S(6)} %select_n.362), kind=kOutput, calls=%fused_computation.32 | convolution fusion | flops 604127232 | bytes 3702788 | tf_op jit(solution)/shard_map/dot_general | solution.py:47
  133.9 3.9 %collective-permute-done.7 = bf16[256,576]{0,1:T(8,128)(2,1)} collective-permute-done((bf16[256,576]{0,1:T(8,128)(2,1)}, bf16[256,576]{0,1:T(8,128)(2,1)}, u32[]{:S(2)}, u32[]{:S(2)}) %collective-permute-start.7) | collective-permute-done | bytes 294944 | tf_op jit(solution)/shard_map/ppermute | solution.py:13
  139.0 2.9 %collective-permute-start.8 = (bf16[256,576]{0,1:T(8,128)(2,1)S(1)}, bf16[256,576]{0,1:T(8,128)(2,1)S(1)}, u32[]{:S(2)}, u32[]{:S(2)}) collective-permute-start(bf16[256,576]{0,1:T(8,128)(2,1)S(1)} %fusion.71), channel_id=1, source_target_pairs={{0,128},{128,0},{1,129},{129,1},{2,130},{130,2},{3,131},{131,3},{4... | collective-permute-start | bytes 884744 | tf_op jit(solution)/shard_map/ppermute | solution.py:100
  145.1 3.1 %collective-permute-start.11 = (bf16[256,576]{0,1:T(8,128)(2,1)S(1)}, bf16[256,576]{0,1:T(8,128)(2,1)S(1)}, u32[]{:S(2)}, u32[]{:S(2)}) collective-permute-start(bf16[256,576]{0,1:T(8,128)(2,1)S(1)} %collective-permute-done.8), channel_id=1, source_target_pairs={{128,160},{160,192},{192,224},{224,128},{129,161},{161,193},{193,2... | collective-permute-start | bytes 884744 | tf_op jit(solution)/shard_map/ppermute | solution.py:15
  148.1 2.2 collective-permute-start.9
  152.9 3.9 %collective-permute-done.9 = bf16[256,576]{0,1:T(8,128)(2,1)S(1)} collective-permute-done((bf16[256,576]{0,1:T(8,128)(2,1)S(1)}, bf16[256,576]{0,1:T(8,128)(2,1)S(1)}, u32[]{:S(2)}, u32[]{:S(2)}) %collective-permute-start.9) | collective-permute-done | bytes 294944 | tf_op jit(solution)/shard_map/ppermute | solution.py:15
  157.1 6.5 %conditional.3 = (bf16[256,2048]{1,0:T(8,128)(2,1)S(1)}) conditional(s32[]{:T(128)} %convert_element_type.88, (bf16[1,2304,2048]{2,1,0:T(8,128)(2,1)}, bf16[256,2304]{0,1:T(8,128)(2,1)S(1)}, f32[1,2048]{1,0:T(1,128)S(1)}, f32[256,2048]{1,0:T(8,128)S(1)}) %tuple.46, () %tuple.23), branch_computations={%region_3.4_spmd, %region_4.5_spmd} | conditional | flops 2418016256 | bytes 13770760 | solution.py:104
  157.3 6.3 %fusion.25 = bf16[256,2048]{1,0:T(8,128)(2,1)S(1)} fusion(f32[256,2048]{1,0:T(8,128)S(1)} %get-tuple-element.29, bf16[256,2304]{0,1:T(8,128)(2,1)S(1)} %get-tuple-element.45, bf16[1,2304,2048]{2,1,0:T(8,128)(2,1)} %get-tuple-element.27, f32[2048]{0:T(1024)S(1)} %bitcast.57), kind=kOutput, calls=%fused_computation.11 | convolution fusion | flops 2418016256 | bytes 13770752 | tf_op jit(solution)/shard_map/cond/branch_0_fun/dot_general | solution.py:68
  165.0 2.2 collective-permute-done.12
  167.3 52.7 %all-gather.5.cloned.1.call-done = bf16[2048,2304]{0,1:T(8,128)(2,1)} async-done(((bf16[2048,72]{0,1:T(8,128)(2,1)}), bf16[2048,2304]{0,1:T(8,128)(2,1)}) %all-gather.5.cloned.1.call-update) | async-done | bytes 9437200 | tf_op jit(solution)/shard_map/all_gather | solution.py:85
  220.0 2.5 fusion.56
  223.7 2.5 fusion.59
  228.1 2.5 fusion.62
  230.7 2.6 %fusion.65 = bf16[256,576]{0,1:T(8,128)(2,1)S(1)} fusion(bf16[256,2048]{1,0:T(8,128)(2,1)S(1)} %broadcast_select_fusion, bf16[2048,2304]{0,1:T(8,128)(2,1)} %all-gather.5.cloned.1.call-done, s32[]{:T(128)S(6)} %select_n.362), kind=kOutput, calls=%fused_computation.36 | convolution fusion | flops 604127232 | bytes 3702788 | tf_op jit(solution)/shard_map/dot_general | solution.py:47
  233.3 2.2 collective-permute-done.14
  235.4 3.1 %collective-permute-done.15 = bf16[256,576]{0,1:T(8,128)(2,1)S(1)} collective-permute-done((bf16[256,576]{0,1:T(8,128)(2,1)S(1)}, bf16[256,576]{0,1:T(8,128)(2,1)S(1)}, u32[]{:S(2)}, u32[]{:S(2)}) %collective-permute-start.15) | collective-permute-done | bytes 294944 | tf_op jit(solution)/shard_map/ppermute | solution.py:13
  238.5 2.1 fusion.72
  241.9 3.9 %collective-permute-done.16 = bf16[256,576]{0,1:T(8,128)(2,1)S(1)} collective-permute-done((bf16[256,576]{0,1:T(8,128)(2,1)S(1)}, bf16[256,576]{0,1:T(8,128)(2,1)S(1)}, u32[]{:S(2)}, u32[]{:S(2)}) %collective-permute-start.16) | collective-permute-done | bytes 294944 | tf_op jit(solution)/shard_map/ppermute | solution.py:113
  (71 shorter events, 30.4 us)
Async XLA Ops:
  7.2 109.4 %all-gather.3.cloned.1.call-start = ((), (), s32[]{:S(2)}) async-start(), calls=%async_computation | async-start | bytes 9732096 | tf_op jit(solution)/shard_map/all_gather | solution.py:84
  7.2 2.2 collective-permute-start.4
  11.2 208.8 %all-gather.5.cloned.1.call-start = ((), (), s32[]{:S(2)}) async-start(), calls=%async_computation.1 | async-start | bytes 9732096 | tf_op jit(solution)/shard_map/all_gather | solution.py:85
  12.0 5.3 %collective-permute-start = (bf16[256,576]{0,1:T(8,128)(2,1)}, bf16[256,576]{0,1:T(8,128)(2,1)S(1)}, u32[]{:S(2)}, u32[]{:S(2)}) collective-permute-start(bf16[256,576]{0,1:T(8,128)(2,1)} %param.13), channel_id=1, source_target_pairs={{0,96},{32,0},{64,32},{96,64},{1,97},{33,1},{65,33},{97,65},{2,98}... | collective-permute-start | bytes 884744 | tf_op jit(solution)/shard_map/ppermute | solution.py:15
  12.7 4.6 %collective-permute-start.1 = (bf16[256,576]{0,1:T(8,128)(2,1)}, bf16[256,576]{0,1:T(8,128)(2,1)S(1)}, u32[]{:S(2)}, u32[]{:S(2)}) collective-permute-start(bf16[256,576]{0,1:T(8,128)(2,1)} %param.13), channel_id=1, source_target_pairs={{0,64},{32,96},{64,0},{96,32},{1,65},{33,97},{65,1},{97,33},{2,66}... | collective-permute-start | bytes 884744 | tf_op jit(solution)/shard_map/ppermute | solution.py:15
  13.4 3.9 %collective-permute-start.2 = (bf16[256,576]{0,1:T(8,128)(2,1)}, bf16[256,576]{0,1:T(8,128)(2,1)S(1)}, u32[]{:S(2)}, u32[]{:S(2)}) collective-permute-start(bf16[256,576]{0,1:T(8,128)(2,1)} %param.13), channel_id=1, source_target_pairs={{0,32},{32,64},{64,96},{96,0},{1,33},{33,65},{65,97},{97,1},{2,34}... | collective-permute-start | bytes 884744 | tf_op jit(solution)/shard_map/ppermute | solution.py:15
  18.2 21.1 %collective-permute-start.3 = (bf16[256,2048]{1,0:T(8,128)(2,1)S(1)}, bf16[256,2048]{1,0:T(8,128)(2,1)}, u32[]{:S(2)}, u32[]{:S(2)}) collective-permute-start(bf16[256,2048]{1,0:T(8,128)(2,1)S(1)} %get-tuple-element.58), channel_id=1, source_target_pairs={{0,128},{1,129},{2,130},{3,131},{4,132},{5,133},{6,134},{7,135},{8... | collective-permute-start | bytes 3145736 | tf_op jit(solution)/shard_map/ppermute | solution.py:95
  120.1 12.5 %collective-permute-start.5 = (bf16[256,576]{0,1:T(8,128)(2,1)}, bf16[256,576]{0,1:T(8,128)(2,1)S(1)}, u32[]{:S(2)}, u32[]{:S(2)}) collective-permute-start(bf16[256,576]{0,1:T(8,128)(2,1)} %fusion.44), channel_id=1, source_target_pairs={{0,64},{32,96},{64,0},{96,32},{1,65},{33,97},{65,1},{97,33},{2,66}... | collective-permute-start | bytes 884744 | tf_op jit(solution)/shard_map/ppermute | solution.py:13
  124.6 9.3 %collective-permute-start.6 = (bf16[256,576]{0,1:T(8,128)(2,1)}, bf16[256,576]{0,1:T(8,128)(2,1)S(1)}, u32[]{:S(2)}, u32[]{:S(2)}) collective-permute-start(bf16[256,576]{0,1:T(8,128)(2,1)} %fusion.47), channel_id=1, source_target_pairs={{0,32},{32,64},{64,96},{96,0},{1,33},{33,65},{65,97},{97,1},{2,34}... | collective-permute-start | bytes 884744 | tf_op jit(solution)/shard_map/ppermute | solution.py:13
  129.6 8.1 %copy-start.1 = (bf16[256,576]{0,1:T(8,128)(2,1)S(1)}, bf16[256,576]{0,1:T(8,128)(2,1)}, u32[]{:S(2)}) copy-start(bf16[256,576]{0,1:T(8,128)(2,1)} %param.15) | copy-start | bytes 884740
  129.6 8.1 %collective-permute-start.7 = (bf16[256,576]{0,1:T(8,128)(2,1)}, bf16[256,576]{0,1:T(8,128)(2,1)}, u32[]{:S(2)}, u32[]{:S(2)}) collective-permute-start(bf16[256,576]{0,1:T(8,128)(2,1)} %fusion.50), channel_id=1, source_target_pairs={{0,96},{32,0},{64,32},{96,64},{1,97},{33,1},{65,33},{97,65},{2,98}... | collective-permute-start | bytes 884744 | tf_op jit(solution)/shard_map/ppermute | solution.py:13
  129.6 8.1 %copy-start.10 = (bf16[1,256,576]{1,2,0:T(8,128)(2,1)S(1)}, bf16[1,256,576]{1,2,0:T(8,128)(2,1)}, u32[]{:S(2)}) copy-start(bf16[1,256,576]{1,2,0:T(8,128)(2,1)} %param.14) | copy-start | bytes 884740
  132.6 24.4 %copy-start.7 = (bf16[256,576]{0,1:T(8,128)(2,1)}, bf16[256,576]{0,1:T(8,128)(2,1)S(1)}, u32[]{:S(2)}) copy-start(bf16[256,576]{0,1:T(8,128)(2,1)S(1)} %fusion.53) | copy-start | bytes 884740
  132.6 24.2 %copy-start.3 = (bf16[256,576]{0,1:T(8,128)(2,1)}, bf16[256,576]{0,1:T(8,128)(2,1)S(1)}, u32[]{:S(2)}) copy-start(bf16[256,576]{0,1:T(8,128)(2,1)S(1)} %collective-permute-done.5) | copy-start | bytes 884740
  133.9 22.9 %copy-start.5 = (bf16[256,576]{0,1:T(8,128)(2,1)}, bf16[256,576]{0,1:T(8,128)(2,1)S(1)}, u32[]{:S(2)}) copy-start(bf16[256,576]{0,1:T(8,128)(2,1)S(1)} %collective-permute-done.6) | copy-start | bytes 884740
  139.0 4.1 %collective-permute-start.8 = (bf16[256,576]{0,1:T(8,128)(2,1)S(1)}, bf16[256,576]{0,1:T(8,128)(2,1)S(1)}, u32[]{:S(2)}, u32[]{:S(2)}) collective-permute-start(bf16[256,576]{0,1:T(8,128)(2,1)S(1)} %fusion.71), channel_id=1, source_target_pairs={{0,128},{128,0},{1,129},{129,1},{2,130},{130,2},{3,131},{131,3},{4... | collective-permute-start | bytes 884744 | tf_op jit(solution)/shard_map/ppermute | solution.py:100
  143.1 9.0 %collective-permute-start.10 = (bf16[256,576]{0,1:T(8,128)(2,1)S(1)}, bf16[256,576]{0,1:T(8,128)(2,1)S(1)}, u32[]{:S(2)}, u32[]{:S(2)}) collective-permute-start(bf16[256,576]{0,1:T(8,128)(2,1)S(1)} %collective-permute-done.8), channel_id=1, source_target_pairs={{128,192},{160,224},{192,128},{224,160},{129,193},{161,225},{193,1... | collective-permute-start | bytes 884744 | tf_op jit(solution)/shard_map/ppermute | solution.py:15
  145.1 7.9 %collective-permute-start.11 = (bf16[256,576]{0,1:T(8,128)(2,1)S(1)}, bf16[256,576]{0,1:T(8,128)(2,1)S(1)}, u32[]{:S(2)}, u32[]{:S(2)}) collective-permute-start(bf16[256,576]{0,1:T(8,128)(2,1)S(1)} %collective-permute-done.8), channel_id=1, source_target_pairs={{128,160},{160,192},{192,224},{224,128},{129,161},{161,193},{193,2... | collective-permute-start | bytes 884744 | tf_op jit(solution)/shard_map/ppermute | solution.py:15
  148.1 8.7 %collective-permute-start.9 = (bf16[256,576]{0,1:T(8,128)(2,1)S(1)}, bf16[256,576]{0,1:T(8,128)(2,1)S(1)}, u32[]{:S(2)}, u32[]{:S(2)}) collective-permute-start(bf16[256,576]{0,1:T(8,128)(2,1)S(1)} %collective-permute-done.8), channel_id=1, source_target_pairs={{128,224},{160,128},{192,160},{224,192},{129,225},{161,129},{193,1... | collective-permute-start | bytes 884744 | tf_op jit(solution)/shard_map/ppermute | solution.py:15
  163.6 3.6 %collective-permute-start.12 = (bf16[256,2048]{1,0:T(8,128)(2,1)S(1)}, bf16[256,2048]{1,0:T(8,128)(2,1)S(1)}, u32[]{:S(2)}, u32[]{:S(2)}) collective-permute-start(bf16[256,2048]{1,0:T(8,128)(2,1)S(1)} %get-tuple-element.59), channel_id=1, source_target_pairs={{128,0},{129,1},{130,2},{131,3},{132,4},{133,5},{134,6},{135,7},{1... | collective-permute-start | bytes 3145736 | tf_op jit(solution)/shard_map/ppermute | solution.py:110
  222.5 10.8 %collective-permute-start.13 = (bf16[256,576]{0,1:T(8,128)(2,1)S(1)}, bf16[256,576]{0,1:T(8,128)(2,1)S(1)}, u32[]{:S(2)}, u32[]{:S(2)}) collective-permute-start(bf16[256,576]{0,1:T(8,128)(2,1)S(1)} %fusion.56), channel_id=1, source_target_pairs={{0,64},{32,96},{64,0},{96,32},{1,65},{33,97},{65,1},{97,33},{2,66}... | collective-permute-start | bytes 884744 | tf_op jit(solution)/shard_map/ppermute | solution.py:13
  226.2 9.2 %collective-permute-start.14 = (bf16[256,576]{0,1:T(8,128)(2,1)S(1)}, bf16[256,576]{0,1:T(8,128)(2,1)S(1)}, u32[]{:S(2)}, u32[]{:S(2)}) collective-permute-start(bf16[256,576]{0,1:T(8,128)(2,1)S(1)} %fusion.59), channel_id=1, source_target_pairs={{0,32},{32,64},{64,96},{96,0},{1,33},{33,65},{65,97},{97,1},{2,34}... | collective-permute-start | bytes 884744 | tf_op jit(solution)/shard_map/ppermute | solution.py:13
  230.6 7.9 %collective-permute-start.15 = (bf16[256,576]{0,1:T(8,128)(2,1)S(1)}, bf16[256,576]{0,1:T(8,128)(2,1)S(1)}, u32[]{:S(2)}, u32[]{:S(2)}) collective-permute-start(bf16[256,576]{0,1:T(8,128)(2,1)S(1)} %fusion.62), channel_id=1, source_target_pairs={{0,96},{32,0},{64,32},{96,64},{1,97},{33,1},{65,33},{97,65},{2,98}... | collective-permute-start | bytes 884744 | tf_op jit(solution)/shard_map/ppermute | solution.py:13
  240.6 5.2 %collective-permute-start.16 = (bf16[256,576]{0,1:T(8,128)(2,1)S(1)}, bf16[256,576]{0,1:T(8,128)(2,1)S(1)}, u32[]{:S(2)}, u32[]{:S(2)}) collective-permute-start(bf16[256,576]{0,1:T(8,128)(2,1)S(1)} %get-tuple-element.48), channel_id=1, source_target_pairs={{0,128},{1,129},{2,130},{3,131},{4,132},{5,133},{6,134},{7,135},{8... | collective-permute-start | bytes 884744 | tf_op jit(solution)/shard_map/ppermute | solution.py:113
  (7 other events, 38.2 us)
Sparse Core Ops, SparseCore 0:
  11.4 105.1 all-gather.2
  119.7 100.2 all-gather.4
where the time goes:
time: 254 us; the launch traced here: 253 us
  waiting for transfers between devices  174 us (69%)
  matrix products  29.4 us (12%)
  starting transfers between devices  23.1 us (9%)
  between operations  14.5 us (6%)
  other arithmetic  10.5 us (4%)
    all_gather x1, waiting for transfers between devices, shards(): first_full = lax.all_gather(first_dec, 'tok', axis=1, tiled=True)  74.9 us
    all_gather x1, waiting for transfers between devices, shards(): second_full = lax.all_gather(second_dec, 'tok', axis=1, tiled=True)  52.7 us
    dot_general x8, matrix products, decode_scatter(): jnp.dot(features, chunk, preferred_element_type=jnp.float32)  23.1 us
    ppermute x1, waiting for transfers between devices, shards(): lax.ppermute(features, 'layer', [(0, 1)])  19.7 us
    ppermute x6, waiting for transfers between devices, within_layer(): lax.ppermute(shard, 'feat', [(i, (i + shift) % n_feat) for i in range(n_f...  10.4 us
    ppermute x6, starting transfers between devices, within_layer(): return lax.ppermute(shard, GROUP, pairs)  9.23 us
    ppermute x6, waiting for transfers between devices, within_layer(): return lax.ppermute(shard, GROUP, pairs)  6.48 us
    dot_general x1, matrix products, encode(): jnp.dot(gathered, enc_weight[0], preferred_element_type=jnp.float32)  6.31 us
  transfers between devices with their start and end apart: 19, of which 14 were waited for; matrix products, arithmetic and copies ran while one was open for 14% of the time, Pallas kernels for 0%

commit v1 on v0

--- a/solution.py
+++ b/solution.py
@@ -82,7 +82,9 @@
     first_dec = jnp.where(first_core, dec_own[0], swapped_next)
     second_dec = jnp.where(first_core, swapped_next, dec_own[0])
     first_full = lax.all_gather(first_dec, "tok", axis=1, tiled=True)
-    second_full = lax.all_gather(second_dec, "tok", axis=1, tiled=True)
+    second_full = jnp.concatenate(
+        lax.all_to_all(jnp.stack([second_dec] * lax.axis_size("tok")), "tok", 0, 0), axis=1
+    )
     mask = feature_mask(block_list, block_count, feat_index, blocks_dev)
     attention = attn_out[0].astype(jnp.float32)
     gathered = feat_gather(resid_in, 0, feat_index, n_feat)

time: 254 us -> 379 us (1.49)
  the two profiles are of different devices: /device:TPU:7 before, /device:TPU:169 now
where the time goes in v1:
time: 379 us
  waiting for transfers between devices  282 us (74%)
  starting transfers between devices  37.2 us (10%)
  matrix products  29.2 us (8%)
  between operations  14.5 us (4%)
  other arithmetic  9.05 us (2%)
  local copies, waits for them, and re-layouts  6.95 us (2%)
    all_gather x1, waiting for transfers between devices, shards(): first_full = lax.all_gather(first_dec, 'tok', axis=1, tiled=True)  233 us
    dot_general x8, matrix products, decode_scatter(): jnp.dot(features, chunk, preferred_element_type=jnp.float32)  22.9 us
    ppermute x1, waiting for transfers between devices, shards(): lax.ppermute(features, 'layer', [(0, 1)])  22 us
    ppermute x6, waiting for transfers between devices, within_layer(): lax.ppermute(shard, 'feat', [(i, (i + shift) % n_feat) for i in range(n_f...  14 us
    ppermute x6, starting transfers between devices, within_layer(): return lax.ppermute(shard, GROUP, pairs)  12.4 us
    all_to_all x1, starting transfers between devices, shards(): lax.all_to_all(jnp.stack([second_dec] * lax.axis_size('tok')), 'tok', 0, 0)  9.07 us
    ppermute x6, starting transfers between devices, within_layer(): lax.ppermute(shard, 'feat', [(i, (i + shift) % n_feat) for i in range(n_f...  8.81 us
  transfers between devices with their start and end apart: 19, of which 12 were waited for; matrix products, arithmetic and copies ran while one was open for 9% of the time, Pallas kernels for 0%

profile of v1, /device:TPU:169, one launch (start us, length us, event | category | flops | bytes accessed | tf_op | source)
XLA Modules:
  0.0 378.6 jit_solution(18389020602089908106)
XLA Ops:
  11.1 4.8 %stack.2 = bf16[32,2048,72]{1,2,0:T(8,128)(2,1)} broadcast(bf16[2048,72]{0,1:T(8,128)(2,1)S(1)} %get-tuple-element.64), dimensions={1,2} | broadcast | bytes 9732096 | tf_op jit(solution)/shard_map/stack | solution.py:86
  16.0 9.1 %all-to-all-start = ((bf16[32,2048,72]{1,2,0:T(8,128)(2,1)}), bf16[32,2048,72]{1,2,0:T(8,128)(2,1)}, u32[]{:S(2)}, u32[]{:S(2)}) async-start(bf16[32,2048,72]{1,2,0:T(8,128)(2,1)} %stack.2), calls=%async_computation | async-start | bytes 18874368 | tf_op jit(solution)/shard_map/all_to_all | solution.py:86
  31.3 22.0 %collective-permute-done.3 = bf16[256,2048]{1,0:T(8,128)(2,1)} collective-permute-done((bf16[256,2048]{1,0:T(8,128)(2,1)S(1)}, bf16[256,2048]{1,0:T(8,128)(2,1)}, u32[]{:S(2)}, u32[]{:S(2)}) %collective-permute-start.3) | collective-permute-done | bytes 1048608 | tf_op jit(solution)/shard_map/ppermute | solution.py:97
  53.3 2.4 broadcast_select_fusion.1
  55.7 233.1 %all-gather.2.cloned.1.call-done = bf16[2048,2304]{0,1:T(8,128)(2,1)} async-done(((bf16[2048,72]{0,1:T(8,128)(2,1)}), bf16[2048,2304]{0,1:T(8,128)(2,1)}) %all-gather.2.cloned.1.call-update) | async-done | bytes 9437200 | tf_op jit(solution)/shard_map/all_gather | solution.py:84
  288.8 3.6 fusion.44
  292.4 3.0 collective-permute-start.5
  295.4 3.3 fusion.47
  298.9 3.3 fusion.50
  302.1 2.5 collective-permute-start.7
  304.6 2.8 fusion.53
  311.5 2.2 collective-permute-start.8
  316.8 6.5 %collective-permute-start.10 = (bf16[256,576]{0,1:T(8,128)(2,1)S(1)}, bf16[256,576]{0,1:T(8,128)(2,1)S(1)}, u32[]{:S(2)}, u32[]{:S(2)}) collective-permute-start(bf16[256,576]{0,1:T(8,128)(2,1)S(1)} %collective-permute-done.8), channel_id=1, source_target_pairs={{128,192},{160,224},{192,128},{224,160},{129,193},{161,225},{193,1... | collective-permute-start | bytes 884744 | tf_op jit(solution)/shard_map/ppermute | solution.py:15
  325.2 3.4 collective-permute-done.10
  331.1 6.3 %conditional.3 = (bf16[256,2048]{1,0:T(8,128)(2,1)S(1)}) conditional(s32[]{:T(128)} %convert_element_type.88, (bf16[1,2304,2048]{2,1,0:T(8,128)(2,1)}, bf16[256,2304]{0,1:T(8,128)(2,1)S(1)}, f32[1,2048]{1,0:T(1,128)S(1)}, f32[256,2048]{1,0:T(8,128)S(1)}) %tuple.46, () %tuple.23), branch_computations={%region_3.4_spmd, %region_4.5_spmd} | conditional | flops 2418016256 | bytes 13770760 | solution.py:106
  331.1 6.3 %fusion.25 = bf16[256,2048]{1,0:T(8,128)(2,1)S(1)} fusion(f32[256,2048]{1,0:T(8,128)S(1)} %get-tuple-element.29, bf16[256,2304]{0,1:T(8,128)(2,1)S(1)} %get-tuple-element.53, bf16[1,2304,2048]{2,1,0:T(8,128)(2,1)} %get-tuple-element.27, f32[2048]{0:T(1024)S(1)} %bitcast.60), kind=kOutput, calls=%fused_computation.11 | convolution fusion | flops 2418016256 | bytes 13770752 | tf_op jit(solution)/shard_map/cond/branch_0_fun/dot_general | solution.py:68
  338.8 2.2 collective-permute-done.12
  341.1 2.5 fusion.62
  343.6 2.5 fusion.59
  346.1 2.5 fusion.56
  351.7 2.5 fusion.65
  354.2 4.2 %collective-permute-done.13 = bf16[256,576]{0,1:T(8,128)(2,1)S(1)} collective-permute-done((bf16[256,576]{0,1:T(8,128)(2,1)S(1)}, bf16[256,576]{0,1:T(8,128)(2,1)S(1)}, u32[]{:S(2)}, u32[]{:S(2)}) %collective-permute-start.13) | collective-permute-done | bytes 294944 | tf_op jit(solution)/shard_map/ppermute | solution.py:13
  358.4 7.0 %collective-permute-done.14 = bf16[256,576]{0,1:T(8,128)(2,1)S(1)} collective-permute-done((bf16[256,576]{0,1:T(8,128)(2,1)S(1)}, bf16[256,576]{0,1:T(8,128)(2,1)S(1)}, u32[]{:S(2)}, u32[]{:S(2)}) %collective-permute-start.14) | collective-permute-done | bytes 294944 | tf_op jit(solution)/shard_map/ppermute | solution.py:13
  368.8 2.2 collective-permute-done.16
  (75 shorter events, 30.4 us)
Async XLA Ops:
  7.2 281.6 %all-gather.2.cloned.1.call-start = ((), (), s32[]{:S(2)}) async-start(), calls=%async_computation.1 | async-start | bytes 9732096 | tf_op jit(solution)/shard_map/all_gather | solution.py:84
  7.2 2.2 collective-permute-start.4
  16.0 325.1 %all-to-all-start = ((bf16[32,2048,72]{1,2,0:T(8,128)(2,1)}), bf16[32,2048,72]{1,2,0:T(8,128)(2,1)}, u32[]{:S(2)}, u32[]{:S(2)}) async-start(bf16[32,2048,72]{1,2,0:T(8,128)(2,1)} %stack.2), calls=%async_computation | async-start | bytes 18874368 | tf_op jit(solution)/shard_map/all_to_all | solution.py:86
  25.1 4.0 %collective-permute-start.2 = (bf16[256,576]{0,1:T(8,128)(2,1)S(1)}, bf16[256,576]{0,1:T(8,128)(2,1)S(1)}, u32[]{:S(2)}, u32[]{:S(2)}) collective-permute-start(bf16[256,576]{0,1:T(8,128)(2,1)S(1)} %copy-done), channel_id=1, source_target_pairs={{0,32},{32,64},{64,96},{96,0},{1,33},{33,65},{65,97},{97,1},{2,34}... | collective-permute-start | bytes 884744 | tf_op jit(solution)/shard_map/ppermute | solution.py:15
  25.7 3.3 collective-permute-start.1
  26.4 2.6 collective-permute-start
  29.9 23.4 %collective-permute-start.3 = (bf16[256,2048]{1,0:T(8,128)(2,1)S(1)}, bf16[256,2048]{1,0:T(8,128)(2,1)}, u32[]{:S(2)}, u32[]{:S(2)}) collective-permute-start(bf16[256,2048]{1,0:T(8,128)(2,1)S(1)} %get-tuple-element.66), channel_id=1, source_target_pairs={{0,128},{1,129},{2,130},{3,131},{4,132},{5,133},{6,134},{7,135},{8... | collective-permute-start | bytes 3145736 | tf_op jit(solution)/shard_map/ppermute | solution.py:97
  292.4 15.1 %collective-permute-start.5 = (bf16[256,576]{0,1:T(8,128)(2,1)}, bf16[256,576]{0,1:T(8,128)(2,1)S(1)}, u32[]{:S(2)}, u32[]{:S(2)}) collective-permute-start(bf16[256,576]{0,1:T(8,128)(2,1)} %fusion.44), channel_id=1, source_target_pairs={{0,64},{32,96},{64,0},{96,32},{1,65},{33,97},{65,1},{97,33},{2,66}... | collective-permute-start | bytes 884744 | tf_op jit(solution)/shard_map/ppermute | solution.py:13
  298.7 10.5 %collective-permute-start.6 = (bf16[256,576]{0,1:T(8,128)(2,1)}, bf16[256,576]{0,1:T(8,128)(2,1)S(1)}, u32[]{:S(2)}, u32[]{:S(2)}) collective-permute-start(bf16[256,576]{0,1:T(8,128)(2,1)} %fusion.47), channel_id=1, source_target_pairs={{0,32},{32,64},{64,96},{96,0},{1,33},{33,65},{65,97},{97,1},{2,34}... | collective-permute-start | bytes 884744 | tf_op jit(solution)/shard_map/ppermute | solution.py:13
  302.1 8.1 %collective-permute-start.7 = (bf16[256,576]{0,1:T(8,128)(2,1)}, bf16[256,576]{0,1:T(8,128)(2,1)}, u32[]{:S(2)}, u32[]{:S(2)}) collective-permute-start(bf16[256,576]{0,1:T(8,128)(2,1)} %fusion.50), channel_id=1, source_target_pairs={{0,96},{32,0},{64,32},{96,64},{1,97},{33,1},{65,33},{97,65},{2,98}... | collective-permute-start | bytes 884744 | tf_op jit(solution)/shard_map/ppermute | solution.py:13
  307.4 23.5 %copy-start.7 = (bf16[256,576]{0,1:T(8,128)(2,1)}, bf16[256,576]{0,1:T(8,128)(2,1)S(1)}, u32[]{:S(2)}) copy-start(bf16[256,576]{0,1:T(8,128)(2,1)S(1)} %fusion.53) | copy-start | bytes 884740
  307.5 23.3 %copy-start.3 = (bf16[256,576]{0,1:T(8,128)(2,1)}, bf16[256,576]{0,1:T(8,128)(2,1)S(1)}, u32[]{:S(2)}) copy-start(bf16[256,576]{0,1:T(8,128)(2,1)S(1)} %collective-permute-done.5) | copy-start | bytes 884740
  309.1 21.6 %copy-start.5 = (bf16[256,576]{0,1:T(8,128)(2,1)}, bf16[256,576]{0,1:T(8,128)(2,1)S(1)}, u32[]{:S(2)}) copy-start(bf16[256,576]{0,1:T(8,128)(2,1)S(1)} %collective-permute-done.6) | copy-start | bytes 884740
  311.5 3.4 collective-permute-start.8
  314.9 10.3 %collective-permute-start.11 = (bf16[256,576]{0,1:T(8,128)(2,1)S(1)}, bf16[256,576]{0,1:T(8,128)(2,1)S(1)}, u32[]{:S(2)}, u32[]{:S(2)}) collective-permute-start(bf16[256,576]{0,1:T(8,128)(2,1)S(1)} %collective-permute-done.8), channel_id=1, source_target_pairs={{128,160},{160,192},{192,224},{224,128},{129,161},{161,193},{193,2... | collective-permute-start | bytes 884744 | tf_op jit(solution)/shard_map/ppermute | solution.py:15
  316.8 11.8 %collective-permute-start.10 = (bf16[256,576]{0,1:T(8,128)(2,1)S(1)}, bf16[256,576]{0,1:T(8,128)(2,1)S(1)}, u32[]{:S(2)}, u32[]{:S(2)}) collective-permute-start(bf16[256,576]{0,1:T(8,128)(2,1)S(1)} %collective-permute-done.8), channel_id=1, source_target_pairs={{128,192},{160,224},{192,128},{224,160},{129,193},{161,225},{193,1... | collective-permute-start | bytes 884744 | tf_op jit(solution)/shard_map/ppermute | solution.py:15
  323.3 7.5 %collective-permute-start.9 = (bf16[256,576]{0,1:T(8,128)(2,1)S(1)}, bf16[256,576]{0,1:T(8,128)(2,1)S(1)}, u32[]{:S(2)}, u32[]{:S(2)}) collective-permute-start(bf16[256,576]{0,1:T(8,128)(2,1)S(1)} %collective-permute-done.8), channel_id=1, source_target_pairs={{128,224},{160,128},{192,160},{224,192},{129,225},{161,129},{193,1... | collective-permute-start | bytes 884744 | tf_op jit(solution)/shard_map/ppermute | solution.py:15
  337.4 3.6 collective-permute-start.12
  348.5 16.9 %copy-start.2 = (bf16[256,576]{0,1:T(8,128)(2,1)S(1)}, bf16[256,576]{0,1:T(8,128)(2,1)}, u32[]{:S(2)}) copy-start(bf16[256,576]{0,1:T(8,128)(2,1)} %param.15) | copy-start | bytes 884740
  348.6 16.9 %copy-start.4 = (bf16[256,576]{0,1:T(8,128)(2,1)S(1)}, bf16[256,576]{0,1:T(8,128)(2,1)}, u32[]{:S(2)}) copy-start(bf16[256,576]{0,1:T(8,128)(2,1)} %copy-done.3) | copy-start | bytes 884740
  348.6 9.8 %collective-permute-start.13 = (bf16[256,576]{0,1:T(8,128)(2,1)S(1)}, bf16[256,576]{0,1:T(8,128)(2,1)S(1)}, u32[]{:S(2)}, u32[]{:S(2)}) collective-permute-start(bf16[256,576]{0,1:T(8,128)(2,1)S(1)} %fusion.56), channel_id=1, source_target_pairs={{0,64},{32,96},{64,0},{96,32},{1,65},{33,97},{65,1},{97,33},{2,66}... | collective-permute-start | bytes 884744 | tf_op jit(solution)/shard_map/ppermute | solution.py:13
  349.0 16.4 %collective-permute-start.14 = (bf16[256,576]{0,1:T(8,128)(2,1)S(1)}, bf16[256,576]{0,1:T(8,128)(2,1)S(1)}, u32[]{:S(2)}, u32[]{:S(2)}) collective-permute-start(bf16[256,576]{0,1:T(8,128)(2,1)S(1)} %fusion.59), channel_id=1, source_target_pairs={{0,32},{32,64},{64,96},{96,0},{1,33},{33,65},{65,97},{97,1},{2,34}... | collective-permute-start | bytes 884744 | tf_op jit(solution)/shard_map/ppermute | solution.py:13
  350.8 14.6 %collective-permute-start.15 = (bf16[256,576]{0,1:T(8,128)(2,1)S(1)}, bf16[256,576]{0,1:T(8,128)(2,1)S(1)}, u32[]{:S(2)}, u32[]{:S(2)}) collective-permute-start(bf16[256,576]{0,1:T(8,128)(2,1)S(1)} %fusion.62), channel_id=1, source_target_pairs={{0,96},{32,0},{64,32},{96,64},{1,97},{33,1},{65,33},{97,65},{2,98}... | collective-permute-start | bytes 884744 | tf_op jit(solution)/shard_map/ppermute | solution.py:13
  367.5 3.5 collective-permute-start.16
  (9 other events, 86.5 us)
Sparse Core Ops, SparseCore 0:
  11.3 277.4 all-gather.1
